TPU v7x, 512 devices: a whole 4x4x16 slice. The times are simulated.
512 devices in a mesh: exp: 16 (over z), sky: 32 (over y, x, core).
Axes of the slice: x: 4, y: 4, z: 16, core: 2. Of those that a mesh axis runs over, the one named last changes fastest.
Arguments:
- sky_start: float32 [16, 128, 4096], P(None, None, 'sky'), may hold values from -6 to 6
- exposures: bfloat16 [16, 1024, 2, 128, 128], P('exp', 'sky'), may hold values from -16 to 16
- weights: bfloat16 [16, 1024, 2], P('exp', 'sky'), may hold values from 0.5 to 2
- footprint_owner: int32 [16, 1024, 1], P('exp', 'sky'), may hold values from 0 to 31; in each aligned block of 32 rows (0 to 31, 32 to 63, ..., all dimensions but the last counted through in order) at most 2 rows name the same one
- footprint_row: int32 [16, 1024], P('exp', 'sky'), may hold values from 0 to 15
- kernel_index: int32 [16, 1024, 2, 2], P('exp', 'sky'), may hold values from 0 to 7
- kernels: bfloat16 [8, 128, 128], replicated, may hold values from -1 to 1
Outputs:
- sky_image: float32 [16, 128, 4096], P(None, None, 'sky')
Inputs may be any that keep to these rules, and one draw needn't show every extreme that they name: `footprint_owner`: the 32 footprint tiles of one device name one tile column at most 2 times, and some tile column exactly 2 times.
All inputs are finite; a program needn't handle non-finite values.
Results may differ from a plain program's by a relative error of at most 0.0035.
Values may be sent and summed in bfloat16 or wider, within the bound.
No kernel may reach another device: no remote copies, remote signals or barrier semaphores. Data moves between devices by JAX's collectives and lax.ppermute only.
A program may use at most 128 MiB of HBM per device.

v0:
```python
import jax
import jax.numpy as jnp
from jax import lax
from jax.sharding import PartitionSpec as P

ITERS = 2
weight_ceiling = 2.0


def padded_2(cells, sides, width):
    for axis, dim in sides:
        count = lax.axis_size(axis)
        ends = count - 1
        head = lax.slice_in_dim(cells, 0, width, axis=dim)
        tail = lax.slice_in_dim(cells, cells.shape[dim] - width, cells.shape[dim], axis=dim)
        cells = jnp.concatenate(
            [
                lax.ppermute(tail, axis, [(i, (i + 1) % count) for i in range(ends)]),
                cells,
                lax.ppermute(head, axis, [((i + 1) % count, i) for i in range(ends)]),
            ],
            axis=dim,
        )
    return cells


def pick_kernels(kernel_ids, kernels):
    table_size = kernels.shape[0]
    tile_edge = kernels.shape[1]
    onehot = (kernel_ids[..., None] == jnp.arange(table_size, dtype=jnp.int32)).astype(jnp.bfloat16)
    onehot = onehot.reshape(-1, table_size)
    selected = jnp.dot(onehot, kernels.reshape(table_size, -1), preferred_element_type=jnp.float32)
    selected = selected.astype(jnp.bfloat16).reshape(kernel_ids.shape + (tile_edge, tile_edge))
    return (selected[..., 0, :, :], selected[..., 1, :, :])


def adjoint_tiles(fetched, left_kernels, right_kernels, tile_weights, observed):
    left_product = jnp.einsum(
        "fetu,fuv->fetv", left_kernels, fetched, preferred_element_type=jnp.float32
    ).astype(jnp.bfloat16)
    predicted = jnp.einsum(
        "fetv,fewv->fetw", left_product, right_kernels, preferred_element_type=jnp.float32
    )
    residual = tile_weights.astype(jnp.float32)[..., None, None] * (
        predicted - observed.astype(jnp.float32)
    )
    residual = residual.astype(jnp.bfloat16)
    back_product = jnp.einsum(
        "feut,feuw->fetw", left_kernels, residual, preferred_element_type=jnp.float32
    ).astype(jnp.bfloat16)
    summed = jnp.sum(
        jnp.einsum(
            "fetw,fewv->fetv", back_product, right_kernels, preferred_element_type=jnp.float32
        ),
        axis=1,
    )
    return summed.astype(jnp.bfloat16)


def laplace_image(padded):
    image_rows = padded.reshape(padded.shape[0] * padded.shape[1], padded.shape[2])
    center = image_rows[:, 1:-1]
    vertical = jnp.pad(center, ((1, 1), (0, 0)))
    laplacian = 4.0 * center - image_rows[:, :-2] - image_rows[:, 2:] - vertical[:-2] - vertical[2:]
    return laplacian.reshape(padded.shape[0], padded.shape[1], padded.shape[2] - 2)


def per_device(
    sky_start, exposures, weights, footprint_owner, footprint_row, kernel_index, kernels
):
    sky_rows = sky_start.shape[0]
    tile_edge = sky_start.shape[1]
    foot_tiles = footprint_row.shape[1]
    expo_count = exposures.shape[2]
    n_sky = lax.axis_size("sky")
    n_exp = lax.axis_size("exp")
    capacity = max(2, 3 * foot_tiles // (2 * n_sky))
    slot_count = n_sky * capacity
    prior_weight = n_exp * foot_tiles * expo_count / (8.0 * sky_rows)
    owner_ids = footprint_owner[0, :, 0]
    tile_rows = footprint_row[0]
    onehot_owner = (owner_ids[:, None] == jnp.arange(n_sky, dtype=jnp.int32)[None, :]).astype(
        jnp.int32
    )
    ranks = jnp.sum((jnp.cumsum(onehot_owner, axis=0) - onehot_owner) * onehot_owner, axis=1)
    slot_of = owner_ids * capacity + ranks
    packing = jnp.arange(slot_count, dtype=jnp.int32)[:, None] == slot_of[None, :]
    requested = jnp.sum(jnp.where(packing, tile_rows[None, :] + 1, 0), axis=1) - 1
    slot_source = jnp.sum(jnp.where(packing, jnp.arange(foot_tiles)[None, :] + 1, 0), axis=1) - 1
    slot_source = jnp.where(slot_source < 0, foot_tiles, slot_source)
    observed = exposures[0]
    tile_weights = weights[0]
    kernel_ids = kernel_index[0]
    incoming = lax.all_to_all(requested, "sky", split_axis=0, concat_axis=0, tiled=True)
    left_kernels, right_kernels = pick_kernels(kernel_ids, kernels)
    receive_map = jnp.arange(sky_rows, dtype=jnp.int32)[:, None] == incoming[None, :]
    local_counts = float(expo_count) * jnp.sum(receive_map.astype(jnp.float32), axis=1)
    receive_half = receive_map.astype(jnp.bfloat16)
    safe_rows = jnp.maximum(incoming, 0)
    rows_per = sky_rows // n_exp
    own_rows = lax.axis_index("exp") * rows_per
    count_block = jnp.broadcast_to(
        local_counts.astype(jnp.bfloat16)[None, :, None], (n_exp, sky_rows, tile_edge)
    )
    half_edge = tile_edge // 2

    def exchange(outgoing_rows, extra, arrived_already=False):
        arrived = outgoing_rows
        if not arrived_already:
            arrived = lax.all_to_all(outgoing_rows, "sky", split_axis=0, concat_axis=0, tiled=True)
        partial_value = jnp.einsum(
            "rj,juv->ruv", receive_half, arrived, preferred_element_type=jnp.float32
        )
        payload = partial_value.astype(jnp.bfloat16).reshape(
            n_exp, rows_per * outgoing_rows.shape[1], tile_edge
        )
        if extra is not None:
            payload = jnp.concatenate([payload, extra], axis=1)
        row_parts = lax.all_to_all(payload, "exp", split_axis=0, concat_axis=0, tiled=True)
        return jnp.sum(row_parts.astype(jnp.float32).reshape((n_exp,) + payload.shape[1:]), axis=0)

    def fetch(part):
        replies = lax.all_to_all(
            part.astype(jnp.bfloat16)[safe_rows], "sky", split_axis=0, concat_axis=0, tiled=True
        )
        return replies[slot_of]

    def gather_scaled(summed, own_denominator):
        piece_edge = summed.shape[0] // rows_per
        own_total = summed.reshape(rows_per, piece_edge, tile_edge)
        scaled = (own_total / own_denominator[:, None, None]).astype(jnp.bfloat16)
        return scaled

    sky_now = sky_start
    fetched = None
    for iteration in range(ITERS):
        if fetched is None:
            fetched = fetch(sky_now)
        adjoint = adjoint_tiles(fetched, left_kernels, right_kernels, tile_weights, observed)
        padded_adjoint = jnp.concatenate(
            [adjoint, jnp.zeros((1, tile_edge, tile_edge), adjoint.dtype)], axis=0
        )
        outgoing = padded_adjoint[slot_source]
        laplacian = laplace_image(padded_2(sky_now, (("sky", 2),), 1))
        if iteration == 0:
            summed = exchange(outgoing[:, :half_edge], count_block)
            counts = summed[rows_per * half_edge :, 0]
            denominator = weight_ceiling * counts + 8.0 * prior_weight
            own_denominator = lax.dynamic_slice_in_dim(denominator, own_rows, rows_per)
            summed_head = summed[: rows_per * half_edge]
            smooth = prior_weight * laplacian / denominator[:, None, None]
        else:
            smooth = prior_weight * laplacian / denominator[:, None, None]
            if iteration + 1 == ITERS:
                scaled = gather_scaled(exchange(outgoing, None), own_denominator)
                gathered = lax.all_gather(scaled, "exp", axis=0, tiled=True)
                sky_now = sky_now - (gathered.astype(jnp.float32) + smooth)
                continue
            summed_head = exchange(outgoing[:, :half_edge], None)
        scaled_head = gather_scaled(summed_head, own_denominator)
        scaled_head, outgoing_tail = lax.optimization_barrier(
            (scaled_head, outgoing[:, half_edge:])
        )
        gathered_head = lax.all_gather(scaled_head, "exp", axis=0, tiled=True)
        arrived_tail = lax.all_to_all(outgoing_tail, "sky", split_axis=0, concat_axis=0, tiled=True)
        gathered_head, arrived_tail = lax.optimization_barrier((gathered_head, arrived_tail))
        scaled_tail = gather_scaled(exchange(arrived_tail, None, True), own_denominator)
        sky_head = sky_now[:, :half_edge] - (
            gathered_head.astype(jnp.float32) + smooth[:, :half_edge]
        )
        if iteration + 1 == ITERS:
            gathered_tail = lax.all_gather(scaled_tail, "exp", axis=0, tiled=True)
            sky_tail = sky_now[:, half_edge:] - (
                gathered_tail.astype(jnp.float32) + smooth[:, half_edge:]
            )
            sky_now = jnp.concatenate([sky_head, sky_tail], axis=1)
            continue
        request_head = sky_head.astype(jnp.bfloat16)[safe_rows]
        request_head, scaled_tail = lax.optimization_barrier((request_head, scaled_tail))
        gathered_tail = lax.all_gather(scaled_tail, "exp", axis=0, tiled=True)
        fetched_head = lax.all_to_all(request_head, "sky", split_axis=0, concat_axis=0, tiled=True)[
            slot_of
        ]
        gathered_tail, fetched_head = lax.optimization_barrier((gathered_tail, fetched_head))
        sky_tail = sky_now[:, half_edge:] - (
            gathered_tail.astype(jnp.float32) + smooth[:, half_edge:]
        )
        fetched = jnp.concatenate([fetched_head, fetch(sky_tail)], axis=1)
        sky_now = jnp.concatenate([sky_head, sky_tail], axis=1)
    return sky_now


def solution(mesh):
    in_specs = (
        P(None, None, "sky"),
        P("exp", "sky", None, None, None),
        P("exp", "sky", None),
        P("exp", "sky", None),
        P("exp", "sky"),
        P("exp", "sky", None, None),
        P(),
    )
    out_specs = P(None, None, "sky")
    return jax.shard_map(
        per_device, mesh=mesh, in_specs=in_specs, out_specs=out_specs, check_vma=False
    )
```

profile of v0, /device:TPU:2, one launch (start us, length us, event | category | flops | bytes accessed | tf_op | source)
XLA Modules:
  0.0 392.2 jit_solution(12822003709473119195)
XLA Ops:
  3.8 9.4 %all-to-all-start = ((s32[32,2,1]{1,2,0:T(1,128)}), s32[32,2,1]{1,2,0:T(1,128)S(1)}, u32[]{:S(2)}, u32[]{:S(2)}) async-start(s32[32,2,1]{1,2,0:T(1,128)} %bitcast.2), calls=%async_computation | async-start | bytes 32768 | tf_op jit(solution)/shard_map/all_to_all | solution.py:94
  13.2 1.3 convert_element_type.137
  14.5 4.9 %all-to-all-done = s32[32,2,1]{1,2,0:T(1,128)S(1)} async-done(((s32[32,2,1]{1,2,0:T(1,128)}), s32[32,2,1]{1,2,0:T(1,128)S(1)}, u32[]{:S(2)}, u32[]{:S(2)}) %all-to-all-start) | async-done | bytes 288 | tf_op jit(solution)/shard_map/all_to_all | solution.py:94
  20.7 2.1 gather_fusion
  22.9 5.2 %all-to-all-start.1 = ((bf16[64,128,128]{2,1,0:T(8,128)(2,1)}), bf16[64,128,128]{2,1,0:T(8,128)(2,1)S(1)}, u32[]{:S(2)}, u32[]{:S(2)}) async-start(bf16[64,128,128]{2,1,0:T(8,128)(2,1)} %gather_fusion), calls=%async_computation.1 | async-start | bytes 4194304 | tf_op jit(solution)/shard_map/all_to_all | solution.py:123
  28.5 1.3 fusion.4
  29.8 3.2 copy.72
  33.0 23.1 %all-to-all-done.1 = bf16[64,128,128]{2,1,0:T(8,128)(2,1)S(1)} async-done(((bf16[64,128,128]{2,1,0:T(8,128)(2,1)}), bf16[64,128,128]{2,1,0:T(8,128)(2,1)S(1)}, u32[]{:S(2)}, u32[]{:S(2)}) %all-to-all-start.1) | async-done | bytes 2097184 | tf_op jit(solution)/shard_map/all_to_all | solution.py:123
  56.8 6.3 %fusion.1 = bf16[32,2,128,128]{3,2,1,0:T(8,128)(2,1)} fusion(bf16[1,32,2,128,128]{4,3,2,1,0:T(8,128)(2,1)} %param.8, f32[32,2]{1,0:T(8,128)S(1)} %copy.43, bf16[32,2,2,128,128]{4,3,2,1,0:T(8,128)(2,1)} %bitcast.93, bf16[32,128,128]{2,1,0:T(8,128)(2,1)S(1)} %gather_fusion.1), kind=kOutput, calls=%fused_computation.12 | convolution fusion | flops 542113792 | bytes 9437440 | tf_op jit(solution)/shard_map/fetv,fewv->fetw/dot_general | solution.py:41
  63.2 4.3 %bitcast_convert_fusion.1 = bf16[32,128,128]{2,1,0:T(8,128)(2,1)S(1)} fusion(bf16[32,2,128,128]{3,2,1,0:T(8,128)(2,1)} %fusion.1, bf16[32,2,2,128,128]{4,3,2,1,0:T(8,128)(2,1)} %bitcast.94), kind=kOutput, calls=%fused_computation.21 | convolution fusion | flops 538443776 | bytes 7340032 | tf_op jit(solution)/shard_map/fetw,fewv->fetv/dot_general | solution.py:52
  67.6 1.0 gather_fusion.2
  68.5 1.5 fusion.72
  70.0 5.9 %all-to-all-start.2 = ((bf16[64,64,128]{2,1,0:T(8,128)(2,1)}), bf16[64,64,128]{2,1,0:T(8,128)(2,1)S(1)}, u32[]{:S(2)}, u32[]{:S(2)}) async-start(bf16[64,64,128]{2,1,0:T(8,128)(2,1)} %get-tuple-element.30), calls=%async_computation.2 | async-start | bytes 2097152 | tf_op jit(solution)/shard_map/all_to_all | solution.py:110
  76.3 15.9 %all-to-all-done.2 = bf16[64,64,128]{2,1,0:T(8,128)(2,1)S(1)} async-done(((bf16[64,64,128]{2,1,0:T(8,128)(2,1)}), bf16[64,64,128]{2,1,0:T(8,128)(2,1)S(1)}, u32[]{:S(2)}, u32[]{:S(2)}) %all-to-all-start.2) | async-done | bytes 1048608 | tf_op jit(solution)/shard_map/all_to_all | solution.py:110
  93.9 13.3 %all-to-all-start.3 = ((bf16[16,80,128]{2,1,0:T(8,128)(2,1)}), bf16[16,80,128]{2,1,0:T(8,128)(2,1)S(1)}, u32[]{:S(2)}, u32[]{:S(2)}) async-start(bf16[16,80,128]{2,1,0:T(8,128)(2,1)} %copy.47), calls=%async_computation.3 | async-start | bytes 655360 | tf_op jit(solution)/shard_map/all_to_all | solution.py:119
  107.2 21.4 %all-to-all-done.3 = bf16[16,80,128]{2,1,0:T(8,128)(2,1)S(1)} async-done(((bf16[16,80,128]{2,1,0:T(8,128)(2,1)}), bf16[16,80,128]{2,1,0:T(8,128)(2,1)S(1)}, u32[]{:S(2)}, u32[]{:S(2)}) %all-to-all-start.3) | async-done | bytes 327712 | tf_op jit(solution)/shard_map/all_to_all | solution.py:119
  129.9 5.6 %all-to-all-start.4 = ((bf16[64,64,128]{2,1,0:T(8,128)(2,1)}), bf16[64,64,128]{2,1,0:T(8,128)(2,1)}, u32[]{:S(2)}, u32[]{:S(2)}) async-start(bf16[64,64,128]{2,1,0:T(8,128)(2,1)} %get-tuple-element.14), calls=%async_computation.4 | async-start | bytes 2097152 | tf_op jit(solution)/shard_map/all_to_all | solution.py:165
  136.3 2.0 collective-permute-start.1
  138.6 2.5 collective-permute-start
  141.1 6.4 %collective-permute-done.1 = f32[16,128,1]{1,0,2:T(8,128)S(1)} collective-permute-done((f32[16,128,1]{1,0,2:T(8,128)S(1)}, f32[16,128,1]{1,0,2:T(8,128)S(1)}, u32[]{:S(2)}, u32[]{:S(2)}) %collective-permute-start.1) | collective-permute-done | bytes 8224 | tf_op jit(solution)/shard_map/ppermute | solution.py:20
  147.5 1.3 copy.51
  148.8 1.4 copy.50
  150.2 2.4 pad_maximum_fusion
  152.6 1.3 slice.118
  153.9 33.8 %all_gather.9 = bf16[16,64,128]{2,1,0:T(8,128)(2,1)} all-gather(bf16[1,64,128]{2,1,0:T(8,128)(2,1)S(1)} %fusion.53), channel_id=1, replica_groups=mesh['exp'=16,'sky'=32] {'exp'}, dimensions={0}, use_global_device_ids=true | all-gather | bytes 278528 | tf_op jit(solution)/shard_map/all_gather | solution.py:164
  187.8 1.9 convolution_convert_fusion.1
  190.5 4.5 %all-to-all-start.5 = ((bf16[16,64,128]{2,1,0:T(8,128)(2,1)}), bf16[16,64,128]{2,1,0:T(8,128)(2,1)S(1)}, u32[]{:S(2)}, u32[]{:S(2)}) async-start(bf16[16,64,128]{2,1,0:T(8,128)(2,1)} %copy.53), calls=%async_computation.5 | async-start | bytes 524288 | tf_op jit(solution)/shard_map/all_to_all | solution.py:119
  194.9 2.5 fusion.36
  199.3 1.6 gather_fusion.3
  201.0 8.2 %all-to-all-done.5 = bf16[16,64,128]{2,1,0:T(8,128)(2,1)S(1)} async-done(((bf16[16,64,128]{2,1,0:T(8,128)(2,1)}), bf16[16,64,128]{2,1,0:T(8,128)(2,1)S(1)}, u32[]{:S(2)}, u32[]{:S(2)}) %all-to-all-start.5) | async-done | bytes 262176 | tf_op jit(solution)/shard_map/all_to_all | solution.py:119
  209.8 7.9 %all-to-all-start.6 = ((bf16[64,64,128]{2,1,0:T(8,128)(2,1)}), bf16[64,64,128]{2,1,0:T(8,128)(2,1)S(1)}, u32[]{:S(2)}, u32[]{:S(2)}) async-start(bf16[64,64,128]{2,1,0:T(8,128)(2,1)} %gather_fusion.3), calls=%async_computation.6 | async-start | bytes 2097152 | tf_op jit(solution)/shard_map/all_to_all | solution.py:181
  217.7 31.1 %all_gather.10 = bf16[16,64,128]{2,1,0:T(8,128)(2,1)S(1)} all-gather(bf16[1,64,128]{2,1,0:T(8,128)(2,1)S(1)} %fusion.52), channel_id=1, replica_groups=mesh['exp'=16,'sky'=32] {'exp'}, dimensions={0}, use_global_device_ids=true | all-gather | bytes 278528 | tf_op jit(solution)/shard_map/all_gather | solution.py:180
  248.8 1.4 gather_fusion.4
  251.9 23.4 %all_to_all.51 = bf16[64,64,128]{2,1,0:T(8,128)(2,1)S(1)} all-to-all(bf16[64,64,128]{2,1,0:T(8,128)(2,1)S(1)} %gather_fusion.5), channel_id=1, replica_groups=mesh['exp'=16,'sky'=32] {'sky'}, dimensions={0} | all-to-all | bytes 2097152 | tf_op jit(solution)/shard_map/all_to_all | solution.py:123
  276.0 6.3 %fusion.3 = bf16[32,2,128,128]{3,2,1,0:T(8,128)(2,1)} fusion(bf16[1,32,2,128,128]{4,3,2,1,0:T(8,128)(2,1)} %param.8, f32[32,2]{1,0:T(8,128)S(1)} %copy.43, bf16[32,2,2,128,128]{4,3,2,1,0:T(8,128)(2,1)} %bitcast.95, bf16[32,64,128]{2,1,0:T(8,128)(2,1)S(1)} %gather_fusion.6, bf16[32,64,128]{2,1,0:T(8,128)(2,1)S(1)} %copy-done.4), kind=kOutput, calls=%fused_computation.14 | convolution fusion | flops 544210944 | bytes 9437440 | tf_op jit(solution)/shard_map/fetv,fewv->fetw/dot_general | solution.py:41
  282.3 4.3 %bitcast_convert_fusion = bf16[32,128,128]{2,1,0:T(8,128)(2,1)S(1)} fusion(bf16[32,2,128,128]{3,2,1,0:T(8,128)(2,1)} %fusion.3, bf16[32,2,2,128,128]{4,3,2,1,0:T(8,128)(2,1)} %bitcast.96), kind=kOutput, calls=%fused_computation.20 | convolution fusion | flops 538443776 | bytes 7340032 | tf_op jit(solution)/shard_map/fetw,fewv->fetv/dot_general | solution.py:52
  286.7 1.0 gather_fusion.7
  287.7 31.9 %all_to_all.52 = bf16[64,128,128]{2,1,0:T(8,128)(2,1)S(1)} all-to-all(bf16[64,128,128]{2,1,0:T(8,128)(2,1)S(1)} %gather_fusion.7), channel_id=1, replica_groups=mesh['exp'=16,'sky'=32] {'sky'}, dimensions={0} | all-to-all | bytes 4194304 | tf_op jit(solution)/shard_map/all_to_all | solution.py:110
  319.6 1.3 fusion.25
  320.8 0.9 copy.56
  321.8 4.3 %all-to-all-start.9 = ((bf16[16,128,128]{2,1,0:T(8,128)(2,1)}), bf16[16,128,128]{2,1,0:T(8,128)(2,1)}, u32[]{:S(2)}, u32[]{:S(2)}) async-start(bf16[16,128,128]{2,1,0:T(8,128)(2,1)} %copy.56), calls=%async_computation.9 | async-start | bytes 1048576 | tf_op jit(solution)/shard_map/all_to_all | solution.py:119
  326.8 3.1 collective-permute-start.3
  330.2 2.1 collective-permute-start.2
  332.7 2.4 collective-permute-done.2
  337.2 18.3 %all-to-all-done.9 = bf16[16,128,128]{2,1,0:T(8,128)(2,1)} async-done(((bf16[16,128,128]{2,1,0:T(8,128)(2,1)}), bf16[16,128,128]{2,1,0:T(8,128)(2,1)}, u32[]{:S(2)}, u32[]{:S(2)}) %all-to-all-start.9) | async-done | bytes 524320 | tf_op jit(solution)/shard_map/all_to_all | solution.py:119
  355.5 1.1 convert_reduce_fusion
  357.2 33.7 %all-gather = bf16[2048,128]{1,0:T(8,128)(2,1)S(1)} all-gather(bf16[128,128]{1,0:T(8,128)(2,1)S(1)} %divide_convert_fusion), channel_id=2, replica_groups=mesh['exp'=16,'sky'=32] {'exp'}, dimensions={0}, use_global_device_ids=true | all-gather | bytes 557056 | tf_op jit(solution)/shard_map/all_gather | solution.py:156
  391.0 1.2 fusion.30
  (76 shorter events, 20.4 us)
Async XLA Ops:
  3.8 15.6 %all-to-all-start = ((s32[32,2,1]{1,2,0:T(1,128)}), s32[32,2,1]{1,2,0:T(1,128)S(1)}, u32[]{:S(2)}, u32[]{:S(2)}) async-start(s32[32,2,1]{1,2,0:T(1,128)} %bitcast.2), calls=%async_computation | async-start | bytes 32768 | tf_op jit(solution)/shard_map/all_to_all | solution.py:94
  22.8 5.3 %copy-start.8 = (bf16[1,32,2]{1,2,0:T(2,128)(2,1)S(1)}, bf16[1,32,2]{1,2,0:T(2,128)(2,1)}, u32[]{:S(2)}) copy-start(bf16[1,32,2]{1,2,0:T(2,128)(2,1)} %param.9) | copy-start | bytes 388
  22.8 5.4 %copy-start.7 = (s32[1,32,2,2]{1,3,2,0:T(2,128)S(1)}, s32[1,32,2,2]{1,3,2,0:T(2,128)}, u32[]{:S(2)}) copy-start(s32[1,32,2,2]{1,3,2,0:T(2,128)} %param.12) | copy-start | bytes 1540
  22.8 5.6 %copy-start.5 = (bf16[8,128,128]{2,1,0:T(8,128)(2,1)S(1)}, bf16[8,128,128]{2,1,0:T(8,128)(2,1)}, u32[]{:S(2)}) copy-start(bf16[8,128,128]{2,1,0:T(8,128)(2,1)} %param.13) | copy-start | bytes 786436
  22.9 33.2 %all-to-all-start.1 = ((bf16[64,128,128]{2,1,0:T(8,128)(2,1)}), bf16[64,128,128]{2,1,0:T(8,128)(2,1)S(1)}, u32[]{:S(2)}, u32[]{:S(2)}) async-start(bf16[64,128,128]{2,1,0:T(8,128)(2,1)} %gather_fusion), calls=%async_computation.1 | async-start | bytes 4194304 | tf_op jit(solution)/shard_map/all_to_all | solution.py:123
  29.8 3.2 copy-start.6
  70.0 22.2 %all-to-all-start.2 = ((bf16[64,64,128]{2,1,0:T(8,128)(2,1)}), bf16[64,64,128]{2,1,0:T(8,128)(2,1)S(1)}, u32[]{:S(2)}, u32[]{:S(2)}) async-start(bf16[64,64,128]{2,1,0:T(8,128)(2,1)} %get-tuple-element.30), calls=%async_computation.2 | async-start | bytes 2097152 | tf_op jit(solution)/shard_map/all_to_all | solution.py:110
  92.9 42.7 %copy-start = (f32[16,128,128]{2,1,0:T(8,128)S(1)}, f32[16,128,128]{2,1,0:T(8,128)}, u32[]{:S(2)}) copy-start(f32[16,128,128]{2,1,0:T(8,128)} %param.7) | copy-start | bytes 3145732
  93.9 34.7 %all-to-all-start.3 = ((bf16[16,80,128]{2,1,0:T(8,128)(2,1)}), bf16[16,80,128]{2,1,0:T(8,128)(2,1)S(1)}, u32[]{:S(2)}, u32[]{:S(2)}) async-start(bf16[16,80,128]{2,1,0:T(8,128)(2,1)} %copy.47), calls=%async_computation.3 | async-start | bytes 655360 | tf_op jit(solution)/shard_map/all_to_all | solution.py:119
  129.9 57.8 %all-to-all-start.4 = ((bf16[64,64,128]{2,1,0:T(8,128)(2,1)}), bf16[64,64,128]{2,1,0:T(8,128)(2,1)}, u32[]{:S(2)}, u32[]{:S(2)}) async-start(bf16[64,64,128]{2,1,0:T(8,128)(2,1)} %get-tuple-element.14), calls=%async_computation.4 | async-start | bytes 2097152 | tf_op jit(solution)/shard_map/all_to_all | solution.py:165
  136.3 11.2 %collective-permute-start.1 = (f32[16,128,1]{1,0,2:T(8,128)S(1)}, f32[16,128,1]{1,0,2:T(8,128)S(1)}, u32[]{:S(2)}, u32[]{:S(2)}) collective-permute-start(f32[16,128,1]{1,0,2:T(8,128)S(1)} %copy.70), channel_id=1, source_target_pairs={{1,0},{2,1},{3,2},{4,3},{5,4},{6,5},{7,6},{8,7},{9,8},{10,9},{11,1... | collective-permute-start | bytes 24584 | tf_op jit(solution)/shard_map/ppermute | solution.py:20
  138.6 10.2 %collective-permute-start = (f32[16,128,1]{1,0,2:T(8,128)S(1)}, f32[16,128,1]{1,0,2:T(8,128)S(1)}, u32[]{:S(2)}, u32[]{:S(2)}) collective-permute-start(f32[16,128,1]{1,0,2:T(8,128)S(1)} %copy.69), channel_id=1, source_target_pairs={{0,1},{1,2},{2,3},{3,4},{4,5},{5,6},{6,7},{7,8},{8,9},{9,10},{10,1... | collective-permute-start | bytes 24584 | tf_op jit(solution)/shard_map/ppermute | solution.py:18
  190.5 18.7 %all-to-all-start.5 = ((bf16[16,64,128]{2,1,0:T(8,128)(2,1)}), bf16[16,64,128]{2,1,0:T(8,128)(2,1)S(1)}, u32[]{:S(2)}, u32[]{:S(2)}) async-start(bf16[16,64,128]{2,1,0:T(8,128)(2,1)} %copy.53), calls=%async_computation.5 | async-start | bytes 524288 | tf_op jit(solution)/shard_map/all_to_all | solution.py:119
  197.5 1.0 copy-start.3
  209.8 39.0 %all-to-all-start.6 = ((bf16[64,64,128]{2,1,0:T(8,128)(2,1)}), bf16[64,64,128]{2,1,0:T(8,128)(2,1)S(1)}, u32[]{:S(2)}, u32[]{:S(2)}) async-start(bf16[64,64,128]{2,1,0:T(8,128)(2,1)} %gather_fusion.3), calls=%async_computation.6 | async-start | bytes 2097152 | tf_op jit(solution)/shard_map/all_to_all | solution.py:181
  251.9 24.1 %copy-start.4 = (bf16[32,64,128]{2,1,0:T(8,128)(2,1)S(1)}, bf16[32,64,128]{2,1,0:T(8,128)(2,1)}, u32[]{:S(2)}) copy-start(bf16[32,64,128]{2,1,0:T(8,128)(2,1)} %gather_fusion.4) | copy-start | bytes 1572868
  319.6 6.5 %copy-start.1 = (f32[16,64,128]{2,1,0:T(8,128)S(1)}, f32[16,64,128]{2,1,0:T(8,128)}, u32[]{:S(2)}) copy-start(f32[16,64,128]{2,1,0:T(8,128)} %get-tuple-element.28) | copy-start | bytes 1572868
  319.6 6.5 %copy-start.2 = (f32[16,64,128]{2,1,0:T(8,128)S(1)}, f32[16,64,128]{2,1,0:T(8,128)}, u32[]{:S(2)}) copy-start(f32[16,64,128]{2,1,0:T(8,128)} %get-tuple-element.26) | copy-start | bytes 1572868
  321.8 33.7 %all-to-all-start.9 = ((bf16[16,128,128]{2,1,0:T(8,128)(2,1)}), bf16[16,128,128]{2,1,0:T(8,128)(2,1)}, u32[]{:S(2)}, u32[]{:S(2)}) async-start(bf16[16,128,128]{2,1,0:T(8,128)(2,1)} %copy.56), calls=%async_computation.9 | async-start | bytes 1048576 | tf_op jit(solution)/shard_map/all_to_all | solution.py:119
  326.8 5.5 %collective-permute-start.3 = (f32[16,128,1]{1,0,2:T(8,128)S(1)}, f32[16,128,1]{1,0,2:T(8,128)S(1)}, u32[]{:S(2)}, u32[]{:S(2)}) collective-permute-start(f32[16,128,1]{1,0,2:T(8,128)S(1)} %copy.58), channel_id=1, source_target_pairs={{1,0},{2,1},{3,2},{4,3},{5,4},{6,5},{7,6},{8,7},{9,8},{10,9},{11,1... | collective-permute-start | bytes 24584 | tf_op jit(solution)/shard_map/ppermute | solution.py:20
  330.2 5.0 %collective-permute-start.2 = (f32[16,128,1]{1,0,2:T(8,128)S(1)}, f32[16,128,1]{1,0,2:T(8,128)S(1)}, u32[]{:S(2)}, u32[]{:S(2)}) collective-permute-start(f32[16,128,1]{1,0,2:T(8,128)S(1)} %copy.57), channel_id=1, source_target_pairs={{0,1},{1,2},{2,3},{3,4},{4,5},{5,6},{6,7},{7,8},{8,9},{9,10},{10,1... | collective-permute-start | bytes 24584 | tf_op jit(solution)/shard_map/ppermute | solution.py:18
where the time goes:
time: 393 us; the launch traced here: 392 us
  blocking collectives  154 us (39%)
  waiting for transfers between devices  100 us (25%)
  starting transfers between devices  65.9 us (17%)
  local copies, waits for them, and re-layouts  26.6 us (7%)
  matrix products  26.3 us (7%)
  other arithmetic  18.5 us (5%)
    all_to_all x3, waiting for transfers between devices, exchange(): lax.all_to_all(payload, 'exp', split_axis=0, concat_axis=0, tiled=True)  47.8 us
    all_gather x1, blocking collectives, per_device(): gathered_head = lax.all_gather(scaled_head, 'exp', axis=0, tiled=True)  33.8 us
    all_gather x1, blocking collectives, per_device(): gathered = lax.all_gather(scaled, 'exp', axis=0, tiled=True)  33.7 us
    all_to_all x1, blocking collectives, exchange(): lax.all_to_all(outgoing_rows, 'sky', split_axis=0, concat_axis=0, tiled=T...  31.9 us
    all_gather x1, blocking collectives, per_device(): gathered_tail = lax.all_gather(scaled_tail, 'exp', axis=0, tiled=True)  31.1 us
    all_to_all x1, blocking collectives, fetch(): lax.all_to_all(part.astype(jnp.bfloat16)[safe_rows], 'sky', split_axis=0,...  23.4 us
    all_to_all x1, waiting for transfers between devices, fetch(): lax.all_to_all(part.astype(jnp.bfloat16)[safe_rows], 'sky', split_axis=0,...  23.1 us
    all_to_all x3, starting transfers between devices, exchange(): lax.all_to_all(payload, 'exp', split_axis=0, concat_axis=0, tiled=True)  22.1 us
  transfers between devices with their start and end apart: 12, of which 8 were waited for; matrix products, arithmetic and copies ran while one was open for 6% of the time, Pallas kernels for 0%

commit v1 on v0

--- a/solution.py
+++ b/solution.py
@@ -153,7 +153,9 @@
             smooth = prior_weight * laplacian / denominator[:, None, None]
             if iteration + 1 == ITERS:
                 scaled = gather_scaled(exchange(outgoing, None), own_denominator)
-                gathered = lax.all_gather(scaled, "exp", axis=0, tiled=True)
+                gathered = jnp.concatenate(
+                    lax.all_to_all(jnp.stack([scaled] * lax.axis_size("exp")), "exp", 0, 0), axis=0
+                )
                 sky_now = sky_now - (gathered.astype(jnp.float32) + smooth)
                 continue
             summed_head = exchange(outgoing[:, :half_edge], None)

time: 393 us -> 397 us (1.010)
  the two profiles are of different devices: /device:TPU:2 before, /device:TPU:32 now
where the time goes in v1:
time: 397 us; the launch traced here: 395 us
  blocking collectives  152 us (38%)
  waiting for transfers between devices  105 us (26%)
  starting transfers between devices  66.3 us (17%)
  local copies, waits for them, and re-layouts  26.7 us (7%)
  matrix products  26.3 us (7%)
  other arithmetic  18.5 us (5%)
    all_to_all x1, blocking collectives, exchange(): lax.all_to_all(payload, 'exp', split_axis=0, concat_axis=0, tiled=True)  36.4 us
    all_to_all x2, waiting for transfers between devices, exchange(): lax.all_to_all(payload, 'exp', split_axis=0, concat_axis=0, tiled=True)  32.8 us
    all_to_all x1, blocking collectives, exchange(): lax.all_to_all(outgoing_rows, 'sky', split_axis=0, concat_axis=0, tiled=T...  31.9 us
    all_gather x1, blocking collectives, per_device(): gathered_head = lax.all_gather(scaled_head, 'exp', axis=0, tiled=True)  31.7 us
    all_gather x1, blocking collectives, per_device(): gathered_tail = lax.all_gather(scaled_tail, 'exp', axis=0, tiled=True)  27.6 us
    all_to_all x1, waiting for transfers between devices, fetch(): lax.all_to_all(part.astype(jnp.bfloat16)[safe_rows], 'sky', split_axis=0,...  25.1 us
    all_to_all x1, blocking collectives, fetch(): lax.all_to_all(part.astype(jnp.bfloat16)[safe_rows], 'sky', split_axis=0,...  24.6 us
    all_to_all x2, starting transfers between devices, exchange(): lax.all_to_all(payload, 'exp', split_axis=0, concat_axis=0, tiled=True)  22.5 us
  transfers between devices with their start and end apart: 12, of which 8 were waited for; matrix products, arithmetic and copies ran while one was open for 6% of the time, Pallas kernels for 0%

profile of v1, /device:TPU:32, one launch (start us, length us, event | category | flops | bytes accessed | tf_op | source)
XLA Modules:
  0.0 395.3 jit_solution(6946295492777257062)
XLA Ops:
  3.8 7.3 %all-to-all-start = ((s32[32,2,1]{1,2,0:T(1,128)}), s32[32,2,1]{1,2,0:T(1,128)S(1)}, u32[]{:S(2)}, u32[]{:S(2)}) async-start(s32[32,2,1]{1,2,0:T(1,128)} %bitcast.2), calls=%async_computation | async-start | bytes 32768 | tf_op jit(solution)/shard_map/all_to_all | solution.py:94
  11.1 1.3 convert_element_type.136
  12.4 6.0 %all-to-all-done = s32[32,2,1]{1,2,0:T(1,128)S(1)} async-done(((s32[32,2,1]{1,2,0:T(1,128)}), s32[32,2,1]{1,2,0:T(1,128)S(1)}, u32[]{:S(2)}, u32[]{:S(2)}) %all-to-all-start) | async-done | bytes 288 | tf_op jit(solution)/shard_map/all_to_all | solution.py:94
  19.7 2.1 gather_fusion
  21.9 4.1 %all-to-all-start.1 = ((bf16[64,128,128]{2,1,0:T(8,128)(2,1)}), bf16[64,128,128]{2,1,0:T(8,128)(2,1)S(1)}, u32[]{:S(2)}, u32[]{:S(2)}) async-start(bf16[64,128,128]{2,1,0:T(8,128)(2,1)} %gather_fusion), calls=%async_computation.1 | async-start | bytes 4194304 | tf_op jit(solution)/shard_map/all_to_all | solution.py:123
  26.3 1.3 fusion.4
  27.6 3.2 copy.74
  30.9 25.1 %all-to-all-done.1 = bf16[64,128,128]{2,1,0:T(8,128)(2,1)S(1)} async-done(((bf16[64,128,128]{2,1,0:T(8,128)(2,1)}), bf16[64,128,128]{2,1,0:T(8,128)(2,1)S(1)}, u32[]{:S(2)}, u32[]{:S(2)}) %all-to-all-start.1) | async-done | bytes 2097184 | tf_op jit(solution)/shard_map/all_to_all | solution.py:123
  56.8 6.3 %fusion.1 = bf16[32,2,128,128]{3,2,1,0:T(8,128)(2,1)} fusion(bf16[1,32,2,128,128]{4,3,2,1,0:T(8,128)(2,1)} %param.8, f32[32,2]{1,0:T(8,128)S(1)} %copy.44, bf16[32,2,2,128,128]{4,3,2,1,0:T(8,128)(2,1)} %bitcast.96, bf16[32,128,128]{2,1,0:T(8,128)(2,1)S(1)} %gather_fusion.1), kind=kOutput, calls=%fused_computation.12 | convolution fusion | flops 542113792 | bytes 9437440 | tf_op jit(solution)/shard_map/fetv,fewv->fetw/dot_general | solution.py:41
  63.1 4.3 %bitcast_convert_fusion.1 = bf16[32,128,128]{2,1,0:T(8,128)(2,1)S(1)} fusion(bf16[32,2,128,128]{3,2,1,0:T(8,128)(2,1)} %fusion.1, bf16[32,2,2,128,128]{4,3,2,1,0:T(8,128)(2,1)} %bitcast.97), kind=kOutput, calls=%fused_computation.21 | convolution fusion | flops 538443776 | bytes 7340032 | tf_op jit(solution)/shard_map/fetw,fewv->fetv/dot_general | solution.py:52
  67.5 1.0 gather_fusion.2
  68.5 1.5 fusion.72
  70.0 3.9 all-to-all-start.2
  74.2 17.0 %all-to-all-done.2 = bf16[64,64,128]{2,1,0:T(8,128)(2,1)S(1)} async-done(((bf16[64,64,128]{2,1,0:T(8,128)(2,1)}), bf16[64,64,128]{2,1,0:T(8,128)(2,1)S(1)}, u32[]{:S(2)}, u32[]{:S(2)}) %all-to-all-start.2) | async-done | bytes 1048608 | tf_op jit(solution)/shard_map/all_to_all | solution.py:110
  92.9 15.2 %all-to-all-start.3 = ((bf16[16,80,128]{2,1,0:T(8,128)(2,1)}), bf16[16,80,128]{2,1,0:T(8,128)(2,1)S(1)}, u32[]{:S(2)}, u32[]{:S(2)}) async-start(bf16[16,80,128]{2,1,0:T(8,128)(2,1)} %copy.48), calls=%async_computation.3 | async-start | bytes 655360 | tf_op jit(solution)/shard_map/all_to_all | solution.py:119
  108.1 20.5 %all-to-all-done.3 = bf16[16,80,128]{2,1,0:T(8,128)(2,1)S(1)} async-done(((bf16[16,80,128]{2,1,0:T(8,128)(2,1)}), bf16[16,80,128]{2,1,0:T(8,128)(2,1)S(1)}, u32[]{:S(2)}, u32[]{:S(2)}) %all-to-all-start.3) | async-done | bytes 327712 | tf_op jit(solution)/shard_map/all_to_all | solution.py:119
  130.0 4.7 %all-to-all-start.4 = ((bf16[64,64,128]{2,1,0:T(8,128)(2,1)}), bf16[64,64,128]{2,1,0:T(8,128)(2,1)}, u32[]{:S(2)}, u32[]{:S(2)}) async-start(bf16[64,64,128]{2,1,0:T(8,128)(2,1)} %get-tuple-element.14), calls=%async_computation.4 | async-start | bytes 2097152 | tf_op jit(solution)/shard_map/all_to_all | solution.py:167
  135.4 2.0 collective-permute-start
  137.7 1.5 collective-permute-start.1
  139.2 1.4 copy.51
  140.5 1.4 collective-permute-done.1
  141.9 1.3 copy.52
  143.2 2.4 pad_maximum_fusion
  145.7 1.3 slice.118
  147.0 31.7 %all_gather.6 = bf16[16,64,128]{2,1,0:T(8,128)(2,1)} all-gather(bf16[1,64,128]{2,1,0:T(8,128)(2,1)S(1)} %fusion.53), channel_id=1, replica_groups=mesh['exp'=16,'sky'=32] {'exp'}, dimensions={0}, use_global_device_ids=true | all-gather | bytes 278528 | tf_op jit(solution)/shard_map/all_gather | solution.py:166
  178.7 1.9 convolution_convert_fusion.1
  181.3 7.3 %all-to-all-start.5 = ((bf16[16,64,128]{2,1,0:T(8,128)(2,1)}), bf16[16,64,128]{2,1,0:T(8,128)(2,1)S(1)}, u32[]{:S(2)}, u32[]{:S(2)}) async-start(bf16[16,64,128]{2,1,0:T(8,128)(2,1)} %copy.54), calls=%async_computation.5 | async-start | bytes 524288 | tf_op jit(solution)/shard_map/all_to_all | solution.py:119
  188.6 2.5 fusion.36
  192.1 0.9 fusion.70
  193.0 1.6 gather_fusion.3
  194.7 12.3 %all-to-all-done.5 = bf16[16,64,128]{2,1,0:T(8,128)(2,1)S(1)} async-done(((bf16[16,64,128]{2,1,0:T(8,128)(2,1)}), bf16[16,64,128]{2,1,0:T(8,128)(2,1)S(1)}, u32[]{:S(2)}, u32[]{:S(2)}) %all-to-all-start.5) | async-done | bytes 262176 | tf_op jit(solution)/shard_map/all_to_all | solution.py:119
  207.7 11.0 %all-to-all-start.6 = ((bf16[64,64,128]{2,1,0:T(8,128)(2,1)}), bf16[64,64,128]{2,1,0:T(8,128)(2,1)S(1)}, u32[]{:S(2)}, u32[]{:S(2)}) async-start(bf16[64,64,128]{2,1,0:T(8,128)(2,1)} %gather_fusion.3), calls=%async_computation.6 | async-start | bytes 2097152 | tf_op jit(solution)/shard_map/all_to_all | solution.py:183
  218.6 27.6 %all_gather.7 = bf16[16,64,128]{2,1,0:T(8,128)(2,1)S(1)} all-gather(bf16[1,64,128]{2,1,0:T(8,128)(2,1)S(1)} %fusion.52), channel_id=1, replica_groups=mesh['exp'=16,'sky'=32] {'exp'}, dimensions={0}, use_global_device_ids=true | all-gather | bytes 278528 | tf_op jit(solution)/shard_map/all_gather | solution.py:182
  246.2 1.4 gather_fusion.4
  247.6 0.9 fusion.68
  249.3 24.6 %all_to_all.56 = bf16[64,64,128]{2,1,0:T(8,128)(2,1)S(1)} all-to-all(bf16[64,64,128]{2,1,0:T(8,128)(2,1)S(1)} %gather_fusion.5), channel_id=1, replica_groups=mesh['exp'=16,'sky'=32] {'sky'}, dimensions={0} | all-to-all | bytes 2097152 | tf_op jit(solution)/shard_map/all_to_all | solution.py:123
  274.6 6.3 %fusion.3 = bf16[32,2,128,128]{3,2,1,0:T(8,128)(2,1)} fusion(bf16[1,32,2,128,128]{4,3,2,1,0:T(8,128)(2,1)} %param.8, f32[32,2]{1,0:T(8,128)S(1)} %copy.44, bf16[32,2,2,128,128]{4,3,2,1,0:T(8,128)(2,1)} %bitcast.98, bf16[32,64,128]{2,1,0:T(8,128)(2,1)S(1)} %gather_fusion.6, bf16[32,64,128]{2,1,0:T(8,128)(2,1)S(1)} %copy-done.4), kind=kOutput, calls=%fused_computation.14 | convolution fusion | flops 544210944 | bytes 9437440 | tf_op jit(solution)/shard_map/fetv,fewv->fetw/dot_general | solution.py:41
  280.9 4.3 %bitcast_convert_fusion = bf16[32,128,128]{2,1,0:T(8,128)(2,1)S(1)} fusion(bf16[32,2,128,128]{3,2,1,0:T(8,128)(2,1)} %fusion.3, bf16[32,2,2,128,128]{4,3,2,1,0:T(8,128)(2,1)} %bitcast.99), kind=kOutput, calls=%fused_computation.20 | convolution fusion | flops 538443776 | bytes 7340032 | tf_op jit(solution)/shard_map/fetw,fewv->fetv/dot_general | solution.py:52
  285.4 1.0 gather_fusion.7
  286.3 31.9 %all_to_all.57 = bf16[64,128,128]{2,1,0:T(8,128)(2,1)S(1)} all-to-all(bf16[64,128,128]{2,1,0:T(8,128)(2,1)S(1)} %gather_fusion.7), channel_id=1, replica_groups=mesh['exp'=16,'sky'=32] {'sky'}, dimensions={0} | all-to-all | bytes 4194304 | tf_op jit(solution)/shard_map/all_to_all | solution.py:110
  318.2 1.3 fusion.25
  319.7 36.4 %all_to_all.58 = bf16[16,128,128]{2,1,0:T(8,128)(2,1)S(1)} all-to-all(bf16[16,128,128]{2,1,0:T(8,128)(2,1)S(1)} %copy.57), channel_id=1, replica_groups=mesh['exp'=16,'sky'=32] {'exp'}, dimensions={0} | all-to-all | bytes 1048576 | tf_op jit(solution)/shard_map/all_to_all | solution.py:119
  357.7 6.6 %all-to-all-start.10 = ((bf16[16,1,128,128]{3,2,1,0:T(8,128)(2,1)}), bf16[16,1,128,128]{3,2,1,0:T(8,128)(2,1)}, u32[]{:S(2)}, u32[]{:S(2)}) async-start(bf16[16,1,128,128]{3,2,1,0:T(8,128)(2,1)} %stack.2), calls=%async_computation.10 | async-start | bytes 1048576 | tf_op jit(solution)/shard_map/all_to_all | solution.py:157
  365.0 1.4 collective-permute-start.2
  366.7 1.3 collective-permute-start.3
  368.4 2.2 collective-permute-done.3
  372.7 20.4 %all-to-all-done.10 = bf16[16,1,128,128]{3,2,1,0:T(8,128)(2,1)} async-done(((bf16[16,1,128,128]{3,2,1,0:T(8,128)(2,1)}), bf16[16,1,128,128]{3,2,1,0:T(8,128)(2,1)}, u32[]{:S(2)}, u32[]{:S(2)}) %all-to-all-start.10) | async-done | bytes 524320 | tf_op jit(solution)/shard_map/all_to_all | solution.py:157
  393.1 2.3 fusion.30
  (77 shorter events, 19.7 us)
Async XLA Ops:
  3.8 14.6 %all-to-all-start = ((s32[32,2,1]{1,2,0:T(1,128)}), s32[32,2,1]{1,2,0:T(1,128)S(1)}, u32[]{:S(2)}, u32[]{:S(2)}) async-start(s32[32,2,1]{1,2,0:T(1,128)} %bitcast.2), calls=%async_computation | async-start | bytes 32768 | tf_op jit(solution)/shard_map/all_to_all | solution.py:94
  21.9 4.2 %copy-start.7 = (s32[1,32,2,2]{1,3,2,0:T(2,128)S(1)}, s32[1,32,2,2]{1,3,2,0:T(2,128)}, u32[]{:S(2)}) copy-start(s32[1,32,2,2]{1,3,2,0:T(2,128)} %param.12) | copy-start | bytes 1540
  21.9 4.4 %copy-start.5 = (bf16[8,128,128]{2,1,0:T(8,128)(2,1)S(1)}, bf16[8,128,128]{2,1,0:T(8,128)(2,1)}, u32[]{:S(2)}) copy-start(bf16[8,128,128]{2,1,0:T(8,128)(2,1)} %param.13) | copy-start | bytes 786436
  21.9 34.1 %all-to-all-start.1 = ((bf16[64,128,128]{2,1,0:T(8,128)(2,1)}), bf16[64,128,128]{2,1,0:T(8,128)(2,1)S(1)}, u32[]{:S(2)}, u32[]{:S(2)}) async-start(bf16[64,128,128]{2,1,0:T(8,128)(2,1)} %gather_fusion), calls=%async_computation.1 | async-start | bytes 4194304 | tf_op jit(solution)/shard_map/all_to_all | solution.py:123
  27.6 3.2 copy-start.8
  27.6 3.3 copy-start.6
  70.0 21.3 %all-to-all-start.2 = ((bf16[64,64,128]{2,1,0:T(8,128)(2,1)}), bf16[64,64,128]{2,1,0:T(8,128)(2,1)S(1)}, u32[]{:S(2)}, u32[]{:S(2)}) async-start(bf16[64,64,128]{2,1,0:T(8,128)(2,1)} %get-tuple-element.30), calls=%async_computation.2 | async-start | bytes 2097152 | tf_op jit(solution)/shard_map/all_to_all | solution.py:110
  91.9 42.7 %copy-start = (f32[16,128,128]{2,1,0:T(8,128)S(1)}, f32[16,128,128]{2,1,0:T(8,128)}, u32[]{:S(2)}) copy-start(f32[16,128,128]{2,1,0:T(8,128)} %param.7) | copy-start | bytes 3145732
  92.9 35.7 %all-to-all-start.3 = ((bf16[16,80,128]{2,1,0:T(8,128)(2,1)}), bf16[16,80,128]{2,1,0:T(8,128)(2,1)S(1)}, u32[]{:S(2)}, u32[]{:S(2)}) async-start(bf16[16,80,128]{2,1,0:T(8,128)(2,1)} %copy.48), calls=%async_computation.3 | async-start | bytes 655360 | tf_op jit(solution)/shard_map/all_to_all | solution.py:119
  130.0 48.7 %all-to-all-start.4 = ((bf16[64,64,128]{2,1,0:T(8,128)(2,1)}), bf16[64,64,128]{2,1,0:T(8,128)(2,1)}, u32[]{:S(2)}, u32[]{:S(2)}) async-start(bf16[64,64,128]{2,1,0:T(8,128)(2,1)} %get-tuple-element.14), calls=%async_computation.4 | async-start | bytes 2097152 | tf_op jit(solution)/shard_map/all_to_all | solution.py:167
  135.4 3.8 collective-permute-start
  137.7 4.2 %collective-permute-start.1 = (f32[16,128,1]{1,0,2:T(8,128)S(1)}, f32[16,128,1]{1,0,2:T(8,128)S(1)}, u32[]{:S(2)}, u32[]{:S(2)}) collective-permute-start(f32[16,128,1]{1,0,2:T(8,128)S(1)} %copy.72), channel_id=1, source_target_pairs={{1,0},{2,1},{3,2},{4,3},{5,4},{6,5},{7,6},{8,7},{9,8},{10,9},{11,1... | collective-permute-start | bytes 24584 | tf_op jit(solution)/shard_map/ppermute | solution.py:20
  181.3 25.7 %all-to-all-start.5 = ((bf16[16,64,128]{2,1,0:T(8,128)(2,1)}), bf16[16,64,128]{2,1,0:T(8,128)(2,1)S(1)}, u32[]{:S(2)}, u32[]{:S(2)}) async-start(bf16[16,64,128]{2,1,0:T(8,128)(2,1)} %copy.54), calls=%async_computation.5 | async-start | bytes 524288 | tf_op jit(solution)/shard_map/all_to_all | solution.py:119
  191.2 1.0 copy-start.3
  207.7 38.6 %all-to-all-start.6 = ((bf16[64,64,128]{2,1,0:T(8,128)(2,1)}), bf16[64,64,128]{2,1,0:T(8,128)(2,1)S(1)}, u32[]{:S(2)}, u32[]{:S(2)}) async-start(bf16[64,64,128]{2,1,0:T(8,128)(2,1)} %gather_fusion.3), calls=%async_computation.6 | async-start | bytes 2097152 | tf_op jit(solution)/shard_map/all_to_all | solution.py:183
  249.3 25.3 %copy-start.4 = (bf16[32,64,128]{2,1,0:T(8,128)(2,1)S(1)}, bf16[32,64,128]{2,1,0:T(8,128)(2,1)}, u32[]{:S(2)}) copy-start(bf16[32,64,128]{2,1,0:T(8,128)(2,1)} %gather_fusion.4) | copy-start | bytes 1572868
  319.5 44.8 %copy-start.1 = (f32[16,64,128]{2,1,0:T(8,128)S(1)}, f32[16,64,128]{2,1,0:T(8,128)}, u32[]{:S(2)}) copy-start(f32[16,64,128]{2,1,0:T(8,128)} %get-tuple-element.28) | copy-start | bytes 1572868
  319.5 44.8 %copy-start.2 = (f32[16,64,128]{2,1,0:T(8,128)S(1)}, f32[16,64,128]{2,1,0:T(8,128)}, u32[]{:S(2)}) copy-start(f32[16,64,128]{2,1,0:T(8,128)} %get-tuple-element.26) | copy-start | bytes 1572868
  357.7 35.4 %all-to-all-start.10 = ((bf16[16,1,128,128]{3,2,1,0:T(8,128)(2,1)}), bf16[16,1,128,128]{3,2,1,0:T(8,128)(2,1)}, u32[]{:S(2)}, u32[]{:S(2)}) async-start(bf16[16,1,128,128]{3,2,1,0:T(8,128)(2,1)} %stack.2), calls=%async_computation.10 | async-start | bytes 1048576 | tf_op jit(solution)/shard_map/all_to_all | solution.py:157
  365.0 3.0 collective-permute-start.2
  366.7 3.9 collective-permute-start.3
